TPU v7x, 32 devices: a whole 2x2x4 slice. The times are simulated.
32 devices in a mesh: vis: 2 (over x), ctx: 8 (over z, y), tp: 2 (over core).
Axes of the slice: x: 2, y: 2, z: 4, core: 2. Of those that a mesh axis runs over, the one named last changes fastest.
Arguments:
- patch_rows: bfloat16 [1024, 1280], P('ctx'), may hold values from -6 to 6
- vit_gain: float32 [1280], replicated, may hold values from 0.25 to 1.75
- vit_bias: float32 [1280], replicated, may hold values from -3 to 3
- vit_qkv: bfloat16 [1280, 3, 16, 80], P(None, None, ('vis', 'tp')), as said below
- vit_out: bfloat16 [16, 80, 1280], P(('vis', 'tp')), may hold values from -0.15625 to 0.15625
- merge_gain: float32 [1280], replicated, may hold values from 0.25 to 1.75
- merge_bias: float32 [1280], replicated, may hold values from -3 to 3
- merge_weight: bfloat16 [5120, 4096], P('ctx', ('vis', 'tp')), may hold values from -0.078125 to 0.078125
- image_patches: int32 [8, 2], replicated, may hold values from 4 to 64, as said below
- window_ids: int32 [1024], P('ctx'), may hold values from 0 to 1023, as said below
- image_pos: int32 [256], replicated, may hold values from 0 to 1023, as said below
- slice_order: int32 [8], replicated, may hold values from 0 to 7, as said below
- doc_ids: int32 [1024], replicated, may hold values from 0 to 3, never falling along the last dimension, each value on 1 to 512 neighbouring positions
- text_rows: bfloat16 [1024, 4096], P('ctx', ('vis', 'tp')), may hold values from -6 to 6
- norm_gain: float32 [4096], replicated, may hold values from 0.25 to 1.75
- w_query: bfloat16 [4096, 8, 4, 128], P(None, 'vis', 'tp'), as said below
- w_keyval: bfloat16 [2, 4096, 8, 128], P('tp', None, 'vis'), as said below
Outputs:
- attention_out: bfloat16 [1024, 8, 512], P('ctx', 'vis', 'tp')
Inputs may be any that keep to these rules, and one draw needn't show every extreme that they name: `image_patches`: each is h * w for an image of h by w patches, h and w even and at most 32; the images of one ctx shard hold at most 128 patches together, exactly 128 on some shard. `window_ids`: equal ids mark one attention window: consecutive slots of one ctx shard, a multiple of 4 of them and at most 64, never in two images; slots after a shard's live patches form windows of 4. `slice_order`: a permutation; ctx shard c holds the sequence slices slice_order[c] and 15 - slice_order[c] of 64 positions, in that order, as its 128 rows. `image_pos`: distinct positions, one for every merged slot, live or not; the 32 slots of any one ctx shard put exactly 4 positions into the rows of each ctx shard. `doc_ids`: never falling along positions; each document holds 1 to 512 positions. `vit_qkv`: independent centred entries. `w_query`: independent centred entries. `w_keyval`: independent centred entries.
All inputs are finite; a program needn't handle non-finite values.
Results may differ from a plain program's by a relative error of at most 0.022.
The roundings to bfloat16 on the way count: a program that leaves them out, or rounds other values in their place, can miss the bound.
Values may be sent and summed in bfloat16 or wider, within the bound.
No kernel may reach another device: no remote copies, remote signals or barrier semaphores. Data moves between devices by JAX's collectives and lax.ppermute only.
A program may use at most 64 MiB of HBM per device.

v0:
```python
import math
import jax
import jax.numpy as jnp
from jax import lax
from jax.sharding import PartitionSpec as P

D = 4096
HD = 128
VD = 1280
VHD = 80
TOK = 128
PCAP = 128
ICAP = 32
norm_eps = 1e-06
rope_base = 1000000.0
big_negative = -1e30


def swapped(value, axis, stride):
    return lax.ppermute(value, axis, [(i, i ^ 1 << stride) for i in range(lax.axis_size(axis))])


def layer_norm(values, scale_vec, shift_vec):
    centre = jnp.mean(values, axis=-1, keepdims=True)
    offset = values - centre
    spread = jnp.mean(offset * offset, axis=-1, keepdims=True)
    return offset * lax.rsqrt(spread + norm_eps) * scale_vec + shift_vec


def rotate(values, positions):
    half_dim = values.shape[-1] // 2
    exponent = jnp.arange(half_dim, dtype=jnp.float32) * (-2.0 / values.shape[-1])
    frequency = jnp.power(jnp.float32(rope_base), exponent)
    angles = positions.astype(jnp.float32)[:, None] * frequency[None, :]
    shape_out = (values.shape[0],) + (1,) * (values.ndim - 2) + (half_dim,)
    cosine = jnp.cos(angles).reshape(shape_out)
    sine_part = jnp.sin(angles).reshape(shape_out)
    lead_half = values[..., :half_dim]
    tail_half = values[..., half_dim:]
    return jnp.concatenate(
        [lead_half * cosine - tail_half * sine_part, tail_half * cosine + lead_half * sine_part],
        axis=-1,
    )


def row_positions(row_ids, slice_order, tokens_dev):
    shards = slice_order.shape[0]
    device_of = row_ids // tokens_dev
    local_row = row_ids % tokens_dev
    half_tok = tokens_dev // 2
    matches = device_of[:, None] == jnp.arange(shards, dtype=jnp.int32)[None, :]
    first_slice = jnp.sum(jnp.where(matches, slice_order[None, :], 0), axis=1)
    slice_ids = jnp.where(local_row < half_tok, first_slice, 2 * shards - 1 - first_slice)
    return slice_ids * half_tok + local_row % half_tok


def place_of(positions, slice_order, tokens_dev):
    shards = slice_order.shape[0]
    half_tok = tokens_dev // 2
    slice_ids = positions // half_tok
    paired = jnp.minimum(slice_ids, 2 * shards - 1 - slice_ids)
    owner_hot = (paired[..., None] == slice_order).astype(jnp.int32)
    owner_dev = jnp.sum(owner_hot * jnp.arange(shards, dtype=jnp.int32), axis=-1)
    local_row = jnp.where(slice_ids < shards, 0, half_tok) + positions % half_tok
    return (owner_dev, local_row, owner_hot)


def local(
    patch_rows,
    vit_gain,
    vit_bias,
    vit_qkv,
    vit_out,
    merge_gain,
    merge_bias,
    merge_weight,
    image_patches,
    window_ids,
    image_pos,
    slice_order,
    doc_ids,
    text_rows,
    norm_gain,
    w_query,
    w_keyval,
):
    shards = lax.axis_size("ctx")
    ctx_index = lax.axis_index("ctx")
    tp_index = lax.axis_index("tp")
    block_feats = merge_weight.shape[0]
    normed = layer_norm(patch_rows.astype(jnp.float32), vit_gain, vit_bias).astype(jnp.bfloat16)
    projected = jnp.einsum(
        "pf,fxhd->pxhd", normed, vit_qkv, preferred_element_type=jnp.float32
    ).astype(jnp.bfloat16)
    scores = jnp.einsum(
        "qhd,khd->hqk", projected[:, 0], projected[:, 1], preferred_element_type=jnp.float32
    ) / math.sqrt(VHD)
    allowed = window_ids[:, None] == window_ids[None, :]
    scores = jnp.where(allowed[None], scores, big_negative)
    powers = jnp.exp(scores - jnp.max(scores, axis=-1, keepdims=True))
    totals = jnp.sum(powers, axis=-1)
    blended = jnp.einsum(
        "hqk,khd->qhd",
        powers.astype(jnp.bfloat16),
        projected[:, 2],
        preferred_element_type=jnp.float32,
    )
    blended = (blended / jnp.transpose(totals)[:, :, None]).astype(jnp.bfloat16)
    branch_part = jnp.einsum("phd,hdf->pf", blended, vit_out, preferred_element_type=jnp.float32)
    branch_sum = lax.psum(branch_part, ("vis", "tp"))
    hidden = patch_rows.astype(jnp.float32) + branch_sum
    merged = layer_norm(hidden, merge_gain, merge_bias).astype(jnp.bfloat16).reshape(ICAP, 4 * VD)
    send_each = ICAP // shards
    slot_ids = jnp.arange(ICAP, dtype=jnp.int32)
    shard_ids = jnp.arange(shards, dtype=jnp.int32)
    live_count = jnp.sum(image_patches, axis=1) // 4
    all_pos = image_pos.reshape(shards, ICAP)
    owner_dev, local_row, owner_hot = place_of(all_pos, slice_order, TOK)
    before = jnp.cumsum(owner_hot, axis=1) - owner_hot
    rank_in = jnp.sum(before * owner_hot, axis=-1)
    is_live = slot_ids[None, :] < live_count[:, None]
    own_hot = (shard_ids == ctx_index)[:, None]
    own_owner = jnp.sum(jnp.where(own_hot, owner_dev, 0), axis=0)
    own_rank = jnp.sum(jnp.where(own_hot, rank_in, 0), axis=0)
    target_slot = own_owner * send_each + own_rank
    picker = (target_slot[None, :] == slot_ids[:, None]).astype(jnp.bfloat16)
    ordered = jnp.dot(picker, merged, preferred_element_type=jnp.float32).astype(jnp.bfloat16)
    blocks = jnp.transpose(ordered.reshape(ICAP, shards, block_feats), (1, 0, 2))
    received = lax.all_to_all(blocks, "ctx", split_axis=0, concat_axis=0, tiled=True)
    by_dest = jnp.transpose(
        received.reshape(shards, shards, send_each, block_feats), (1, 0, 2, 3)
    ).reshape(shards * ICAP, block_feats)
    partial = jnp.dot(by_dest, merge_weight, preferred_element_type=jnp.float32)
    incoming = lax.psum_scatter(partial, "ctx", scatter_dimension=0, tiled=True).astype(
        jnp.bfloat16
    )
    mine_live = ((owner_dev == ctx_index) & is_live).reshape(-1)
    column_of = (shard_ids[:, None] * send_each + rank_in).reshape(-1)
    row_hot = (
        (local_row.reshape(-1)[None, :] == jnp.arange(TOK, dtype=jnp.int32)[:, None])
        & mine_live[None, :]
    ).astype(jnp.bfloat16)
    column_hot = (column_of[:, None] == slot_ids[None, :]).astype(jnp.bfloat16)
    placing = jnp.dot(row_hot, column_hot, preferred_element_type=jnp.float32)
    is_image = jnp.sum(placing, axis=1) > 0.5
    image_part = jnp.dot(placing.astype(jnp.bfloat16), incoming, preferred_element_type=jnp.float32)
    embeds = jnp.where(is_image[:, None], image_part.astype(jnp.bfloat16), text_rows)
    full_rows = lax.all_gather(embeds, ("vis", "tp"), axis=1, tiled=True)
    widened = full_rows.astype(jnp.float32)
    normed_rows = (
        widened
        * lax.rsqrt(jnp.mean(widened * widened, axis=1, keepdims=True) + norm_eps)
        * norm_gain
    ).astype(jnp.bfloat16)
    own_positions = row_positions(
        ctx_index * TOK + jnp.arange(TOK, dtype=jnp.int32), slice_order, TOK
    )
    own_doc = jnp.take(doc_ids, own_positions)
    kv_heads = w_query.shape[1]
    groups = w_query.shape[2]
    queries = jnp.einsum("td,dhgk->thgk", normed_rows, w_query, preferred_element_type=jnp.float32)
    queries = rotate(queries, own_positions).astype(jnp.bfloat16)
    projected_half = jnp.einsum(
        "td,dhk->thk", normed_rows, w_keyval[0], preferred_element_type=jnp.float32
    )
    own_half = jnp.where(
        tp_index == 0, rotate(projected_half, own_positions), projected_half
    ).astype(jnp.bfloat16)
    both = lax.all_gather(own_half, ("ctx", "tp"), axis=0, tiled=False).reshape(
        shards, 2, TOK, kv_heads, HD
    )
    key_count = shards * TOK
    keys_every = both[:, 0].reshape(key_count, kv_heads, HD)
    values_every = both[:, 1].reshape(key_count, kv_heads, HD)
    key_pos = row_positions(jnp.arange(key_count, dtype=jnp.int32), slice_order, TOK)
    key_doc = jnp.take(doc_ids, key_pos)
    allowed_now = (key_pos[None, :] <= own_positions[:, None]) & (
        key_doc[None, :] == own_doc[:, None]
    )
    scores_now = jnp.einsum(
        "qkgd,nkd->kgqn", queries, keys_every, preferred_element_type=jnp.float32
    ) / math.sqrt(HD)
    scores_now = jnp.where(allowed_now[None, None], scores_now, big_negative)
    best = jnp.max(scores_now, axis=-1, keepdims=True)
    powers_now = jnp.exp(scores_now - best)
    total_final = jnp.sum(powers_now, axis=-1)
    accum_final = jnp.einsum(
        "kgqn,nkd->kgqd",
        powers_now.astype(jnp.bfloat16),
        values_every,
        preferred_element_type=jnp.float32,
    )
    result = accum_final / total_final[..., None]
    return (
        jnp.transpose(result, (2, 0, 1, 3)).reshape(TOK, kv_heads, groups * HD).astype(jnp.bfloat16)
    )


def solution(mesh):
    placed = (
        P("ctx", None),
        P(),
        P(),
        P(None, None, ("vis", "tp"), None),
        P(("vis", "tp"), None, None),
        P(),
        P(),
        P("ctx", ("vis", "tp")),
        P(),
        P("ctx"),
        P(),
        P(),
        P(),
        P("ctx", ("vis", "tp")),
        P(),
        P(None, "vis", "tp", None),
        P("tp", None, "vis", None),
    )
    return jax.shard_map(
        local, mesh=mesh, in_specs=placed, out_specs=P("ctx", "vis", "tp"), check_vma=False
    )
```

profile of v0, /device:TPU:0, one launch (start us, length us, event | category | flops | bytes accessed | tf_op | source)
XLA Modules:
  0.0 236.7 jit_solution(16527992637986011291)
XLA Ops:
  6.6 1.2 convert_reduce_fusion
  7.9 1.2 fusion.28
  9.1 1.9 fusion.32
  11.0 0.1 broadcast_compare_fusion
  11.1 0.3 fusion.96
  11.5 2.6 %convolution_bitcast_fusion = f32[128,1280]{1,0:T(8,128)} fusion(bf16[4,80,1280]{2,1,0:T(8,128)(2,1)} %param.21, f32[4,128,128]{1,2,0:T(8,128)S(1)} %get-tuple-element.22, f32[4,128]{1,0:T(4,128)S(1)} %get-tuple-element.21, bf16[128,3,4,80]{0,3,2,1:T(8,128)(2,1)S(1)} %convert_element_type.68, f32[128,4]{0,1:T(4,128)S(1)} %bitcast.111), kind=kOutput, calls=%fused_computation.10 | convolution fusion | flops 115556352 | bytes 1822720 | tf_op jit(solution)/shard_map/phd,hdf->pf/dot_general | solution.py:109
  14.3 0.7 fusion.50
  15.0 0.7 fusion.94
  15.7 0.1 select_reduce_fusion.2
  15.9 35.1 %all-reduce.2.cloned.1.call-done = f32[128,1280]{1,0:T(8,128)} async-done(((f32[128,1280]{1,0:T(8,128)}), f32[128,1280]{1,0:T(8,128)}) %all-reduce.2.cloned.1.call-update) | async-done | bytes 655376 | tf_op jit(solution)/shard_map/psum | solution.py:110
  51.0 1.2 fusion.47
  52.2 1.3 multiply_reduce_fusion
  53.6 1.3 add_convert_fusion
  54.9 0.2 reshape.665
  55.1 0.2 convolution_convert_fusion
  55.4 15.4 %all_to_all.5 = bf16[8,32,640]{2,1,0:T(8,128)(2,1)S(1)} all-to-all(bf16[8,32,640]{2,1,0:T(8,128)(2,1)S(1)} %bitcast.102), channel_id=1, replica_groups=mesh['vis'=2,'ctx'=8,'tp'=2] {'ctx'}, dimensions={0} | all-to-all | bytes 655360 | tf_op jit(solution)/shard_map/all_to_all | solution.py:129
  70.7 0.1 copy.88
  70.8 0.1 copy.89
  71.0 2.9 %fusion.97 = f32[256,1024]{1,0:T(8,128)} fusion(bf16[256,640]{1,0:T(8,128)(2,1)S(1)} %reshape.668, bf16[640,1024]{1,0:T(8,128)(2,1)} %param.24), kind=kOutput, calls=%fused_computation.190 | convolution fusion | flops 335544320 | bytes 2686976 | tf_op jit(solution)/shard_map/dot_general | solution.py:133
  74.3 0.1 and.279
  74.5 0.3 fusion.95
  74.8 61.8 %reduce-scatter.2.cloned.1.call-done = f32[32,1024]{1,0:T(8,128)} async-done(((f32[256,1024]{1,0:T(8,128)}), f32[32,1024]{1,0:T(8,128)}) %reduce-scatter.2.cloned.1.call-update) | async-done | bytes 131088 | tf_op jit(solution)/shard_map/reduce_scatter | solution.py:134
  136.6 1.9 fusion.16
  138.5 0.2 all-gather.6.cloned.1.call-start
  138.7 0.1 select_reduce_fusion.3
  138.9 1.0 gather_fusion.1
  139.9 0.5 and_select_fusion.8
  140.4 7.6 %copy.90 = bf16[4096,4,128]{0,2,1:T(8,128)(2,1)} copy(bf16[4096,4,128]{2,1,0:T(4,128)(2,1)} %bitcast.97) | data formatting | bytes 8388608 | tf_op jit(solution)/shard_map/squeeze | solution.py:164
  148.0 0.2 multiply_cosine_fusion
  148.2 6.1 %all-gather.4.cloned.1.call-done = bf16[128,4096]{1,0:T(8,128)(2,1)} async-done(((bf16[128,1024]{1,0:T(8,128)(2,1)}), bf16[128,4096]{1,0:T(8,128)(2,1)}) %all-gather.4.cloned.1.call-update) | async-done | bytes 1048592 | tf_op jit(solution)/shard_map/all_gather | solution.py:148
  154.3 1.5 fusion.3
  155.9 3.8 %fusion.40 = f32[128,512]{0,1:S(1)} fusion(bf16[4096,512]{0,1:T(8,128)(2,1)} %bitcast.98, bf16[128,4096]{1,0:T(8,128)(2,1)} %all-gather.4.cloned.1.call-done, f32[4096]{0:T(1024)S(1)} %copy-done.8, f32[128]{0:T(128)S(1)} %add_rsqrt_fusion), kind=kOutput, calls=%fused_computation.50 | convolution fusion | flops 538968064 | bytes 5521920
  159.8 0.7 fusion.42
  160.5 21.3 %copy.92 = bf16[4096,4,2,128]{0,3,2,1:T(8,128)(2,1)} copy(bf16[4096,4,2,128]{3,2,1,0:T(2,128)(2,1)} %param.32) | data formatting | bytes 16777216 | tf_op args[15]
  181.8 0.1 select_reduce_fusion
  181.9 4.5 %gather_fusion = s32[1024]{0:T(1024)S(1)} fusion(s32[1024]{0:T(1024)S(1)} %copy-done.1, s32[1024]{0:T(1024)S(1)} %broadcast_clamp_fusion), kind=kCustom, calls=%fused_computation | custom fusion | bytes 12288 | tf_op jit(solution)/shard_map/jit(_take)/gather | solution.py:176
  186.5 1.7 compare_and_fusion
  188.2 5.8 %fusion.38 = f32[128,1024]{0,1:S(1)} fusion(bf16[4096,1024]{0,1:T(8,128)(2,1)} %bitcast.96, bf16[128,4096]{1,0:T(8,128)(2,1)S(1)} %copy-done.3, f32[4096]{0:T(1024)} %param.31, f32[128]{0:T(128)} %copy-done.13), kind=kOutput, calls=%fused_computation.49 | convolution fusion | flops 1075838976 | bytes 9978368
  194.0 0.8 subtract_convert_fusion
  194.8 6.9 %all-gather.6.cloned.1.call-done = bf16[2048,4,128]{0,2,1:T(8,128)(2,1)} async-done(((bf16[128,4,128]{0,2,1:T(8,128)(2,1)}), bf16[2048,4,128]{0,2,1:T(8,128)(2,1)}) %all-gather.6.cloned.1.call-update) | async-done | bytes 2097168 | tf_op jit(solution)/shard_map/all_gather | solution.py:169
  201.7 4.4 %reshape.669 = bf16[8,2,128,4,128]{2,1,0,4,3:T(2,128)(2,1)} reshape(bf16[2048,4,128]{0,2,1:T(8,128)(2,1)} %all-gather.6.cloned.1.call-done) | data formatting | bytes 4194304 | tf_op jit(solution)/shard_map/reshape | solution.py:169
  206.1 6.8 %fusion.93 = (bf16[8,1,128,4,128]{2,1,0,4,3:T(2,128)(2,1)}, bf16[8,1,128,4,128]{2,1,0,4,3:T(2,128)(2,1)}) fusion(bf16[8,2,128,4,128]{2,1,0,4,3:T(2,128)(2,1)} %reshape.669), kind=kLoop, calls=%fused_computation.186 | loop fusion | bytes 4194304 | tf_op jit(solution)/shard_map/slice | solution.py:173
  212.9 5.8 %copy.91 = bf16[8,1,128,4,128]{4,2,0,3,1:T(8,128)(2,1)} copy(bf16[8,1,128,4,128]{2,1,0,4,3:T(2,128)(2,1)} %get-tuple-element.11) | data formatting | bytes 2097152 | tf_op jit(solution)/shard_map/slice | solution.py:173
  218.7 4.7 %copy.105 = bf16[8,1,128,4,128]{4,2,0,3,1:T(8,128)(2,1)S(1)} copy(bf16[8,1,128,4,128]{2,1,0,4,3:T(2,128)(2,1)} %get-tuple-element.12) | data formatting | bytes 2097152
  223.4 2.1 fusion.2
  225.5 0.9 fusion
  226.4 1.9 fusion.23
  228.3 1.8 copy.97
  (75 shorter events, 1.2 us)
Async XLA Ops:
  6.5 2.5 %copy-start = (bf16[1280,3,4,80]{0,3,2,1:T(8,128)(2,1)S(1)}, bf16[1280,3,4,80]{0,3,2,1:T(8,128)(2,1)}, u32[]{:S(2)}) copy-start(bf16[1280,3,4,80]{0,3,2,1:T(8,128)(2,1)} %param.20) | copy-start | bytes 7372804
  6.5 44.5 %copy-start.2 = (bf16[128,1280]{1,0:T(8,128)(2,1)S(1)}, bf16[128,1280]{1,0:T(8,128)(2,1)}, u32[]{:S(2)}) copy-start(bf16[128,1280]{1,0:T(8,128)(2,1)} %param.17) | copy-start | bytes 983044
  6.5 4.5 %copy-start.15 = (s32[128]{0:T(128)S(1)}, s32[128]{0:T(128)}, u32[]{:S(2)}) copy-start(s32[128]{0:T(128)} %param.26) | copy-start | bytes 1540
  6.5 7.6 %copy-start.12 = (s32[256]{0:T(256)S(1)}, s32[256]{0:T(256)}, u32[]{:S(2)}) copy-start(s32[256]{0:T(256)} %param.27) | copy-start | bytes 3076
  6.5 7.7 %copy-start.11 = (s32[8]{0:T(128)S(1)}, s32[8]{0:T(128)}, u32[]{:S(2)}) copy-start(s32[8]{0:T(128)} %param.28) | copy-start | bytes 100
  6.5 44.4 %all-reduce.2.cloned.1.call-start = ((), (), s32[]{:S(2)}) async-start(), calls=%async_computation.2 | async-start | bytes 1310720 | tf_op jit(solution)/shard_map/psum | solution.py:110
  9.1 44.5 %copy-start.9 = (f32[1280]{0:T(1024)S(1)}, f32[1280]{0:T(1024)}, u32[]{:S(2)}) copy-start(f32[1280]{0:T(1024)} %param.23) | copy-start | bytes 15364
  9.1 44.5 %copy-start.10 = (f32[1280]{0:T(1024)S(1)}, f32[1280]{0:T(1024)}, u32[]{:S(2)}) copy-start(f32[1280]{0:T(1024)} %param.22) | copy-start | bytes 15364
  14.0 122.6 %reduce-scatter.2.cloned.1.call-start = ((), (), s32[]{:S(2)}) async-start(), calls=%async_computation.3 | async-start | bytes 1179648 | tf_op jit(solution)/shard_map/reduce_scatter | solution.py:134
  54.8 19.3 %copy-start.16 = (s32[8,2]{0,1:T(2,128)S(1)}, s32[8,2]{0,1:T(2,128)}, u32[]{:S(2)}) copy-start(s32[8,2]{0,1:T(2,128)} %param.25) | copy-start | bytes 196
  54.9 81.8 %copy-start.7 = (bf16[128,1024]{1,0:T(8,128)(2,1)S(1)}, bf16[128,1024]{1,0:T(8,128)(2,1)}, u32[]{:S(2)}) copy-start(bf16[128,1024]{1,0:T(8,128)(2,1)} %param.30) | copy-start | bytes 786436
  55.3 83.6 %copy-start.1 = (s32[1024]{0:T(1024)S(1)}, s32[1024]{0:T(1024)}, u32[]{:S(2)}) copy-start(s32[1024]{0:T(1024)} %param.29) | copy-start | bytes 12292
  74.0 80.3 %all-gather.4.cloned.1.call-start = ((), (), s32[]{:S(2)}) async-start(), calls=%async_computation.4 | async-start | bytes 1310720 | tf_op jit(solution)/shard_map/all_gather | solution.py:148
  138.5 63.2 %all-gather.6.cloned.1.call-start = ((), (), s32[]{:S(2)}) async-start(), calls=%async_computation.5 | async-start | bytes 2228224 | tf_op jit(solution)/shard_map/all_gather | solution.py:169
  140.4 7.6 %copy-start.14 = (s32[128]{0:T(128)}, s32[128]{0:T(128)S(1)}, u32[]{:S(2)}) copy-start(s32[128]{0:T(128)S(1)} %get-tuple-element.10) | copy-start | bytes 1540
  140.4 15.5 %copy-start.8 = (f32[4096]{0:T(1024)S(1)}, f32[4096]{0:T(1024)}, u32[]{:S(2)}) copy-start(f32[4096]{0:T(1024)} %param.31) | copy-start | bytes 49156
  148.2 12.3 %copy-start.5 = (f32[128,64]{0,1:T(8,128)}, f32[128,64]{0,1:T(8,128)S(1)}, u32[]{:S(2)}) copy-start(f32[128,64]{0,1:T(8,128)S(1)} %get-tuple-element.18) | copy-start | bytes 98308
  155.8 26.0 %copy-start.13 = (f32[128]{0:T(128)}, f32[128]{0:T(128)S(1)}, u32[]{:S(2)}) copy-start(f32[128]{0:T(128)S(1)} %add_rsqrt_fusion) | copy-start | bytes 1540
  181.8 6.3 %copy-start.3 = (bf16[128,4096]{1,0:T(8,128)(2,1)S(1)}, bf16[128,4096]{1,0:T(8,128)(2,1)}, u32[]{:S(2)}) copy-start(bf16[128,4096]{1,0:T(8,128)(2,1)} %all-gather.4.cloned.1.call-done) | copy-start | bytes 3145732
  188.2 5.8 %copy-start.6 = (f32[128,64]{0,1:T(8,128)S(1)}, f32[128,64]{0,1:T(8,128)}, u32[]{:S(2)}) copy-start(f32[128,64]{0,1:T(8,128)} %copy-done.5) | copy-start | bytes 98308
  223.4 2.1 copy-start.4
Sparse Core Ops, SparseCore 0:
  14.2 36.7 all-reduce.1
  74.1 62.4 reduce-scatter.1
  138.6 15.6 all-gather.3
  160.6 41.0 all-gather.5
where the time goes:
time: 238 us; the launch traced here: 237 us
  waiting for transfers between devices  110 us (46%)
  local copies, waits for them, and re-layouts  59.1 us (25%)
  matrix products  23.6 us (10%)
  blocking collectives  15.4 us (6%)
  other arithmetic  14.8 us (6%)
  between operations  13.5 us (6%)
    reduce_scatter x1, waiting for transfers between devices, local(): lax.psum_scatter(partial, 'ctx', scatter_dimension=0, tiled=True)  61.8 us
    psum x1, waiting for transfers between devices, local(): branch_sum = lax.psum(branch_part, ('vis', 'tp'))  35.1 us
    unnamed x36, local copies, waits for them, and re-layouts  26.1 us
    all_to_all x1, blocking collectives, local(): lax.all_to_all(blocks, 'ctx', split_axis=0, concat_axis=0, tiled=True)  15.4 us
    slice x2, local copies, waits for them, and re-layouts, local(): keys_every = both[:, 0].reshape(key_count, kv_heads, HD)  12.6 us
    unnamed x3, matrix products  11.6 us
    squeeze x1, local copies, waits for them, and re-layouts, local(): w_keyval[0]  7.62 us
    all_gather x1, waiting for transfers between devices, local(): lax.all_gather(own_half, ('ctx', 'tp'), axis=0, tiled=False)  6.88 us
  transfers between devices with their start and end apart: 4, of which 4 were waited for; matrix products, arithmetic and copies ran while one was open for 20% of the time, Pallas kernels for 0%

commit v1 on v0

--- a/solution.py
+++ b/solution.py
@@ -107,7 +107,7 @@
     )
     blended = (blended / jnp.transpose(totals)[:, :, None]).astype(jnp.bfloat16)
     branch_part = jnp.einsum("phd,hdf->pf", blended, vit_out, preferred_element_type=jnp.float32)
-    branch_sum = lax.psum(branch_part, ("vis", "tp"))
+    branch_sum = jnp.sum(lax.all_gather(branch_part, ("vis", "tp")), axis=0)
     hidden = patch_rows.astype(jnp.float32) + branch_sum
     merged = layer_norm(hidden, merge_gain, merge_bias).astype(jnp.bfloat16).reshape(ICAP, 4 * VD)
     send_each = ICAP // shards

time: 238 us -> 231 us (0.971)
  waiting for transfers between devices: 110 us -> 101 us
    psum x1 -> x0, waiting for transfers between devices: 35.1 us -> none  [local(): branch_sum = lax.psum(branch_part, ('vis', 'tp'))]
    all_gather x0 -> x1, waiting for transfers between devices: none -> 26.6 us  [local(): branch_sum = jnp.sum(lax.all_gather(branch_part, ('vis', 'tp')), axis=0)]
where the time goes in v1:
time: 231 us; the launch traced here: 229 us
  waiting for transfers between devices  101 us (44%)
  local copies, waits for them, and re-layouts  60.1 us (26%)
  matrix products  23.6 us (10%)
  blocking collectives  16.6 us (7%)
  other arithmetic  14.2 us (6%)
  between operations  13.5 us (6%)
    reduce_scatter x1, waiting for transfers between devices, local(): lax.psum_scatter(partial, 'ctx', scatter_dimension=0, tiled=True)  61.3 us
    all_gather x1, waiting for transfers between devices, local(): branch_sum = jnp.sum(lax.all_gather(branch_part, ('vis', 'tp')), axis=0)  26.6 us
    unnamed x36, local copies, waits for them, and re-layouts  26.1 us
    all_to_all x1, blocking collectives, local(): lax.all_to_all(blocks, 'ctx', split_axis=0, concat_axis=0, tiled=True)  16.6 us
    slice x2, local copies, waits for them, and re-layouts, local(): keys_every = both[:, 0].reshape(key_count, kv_heads, HD)  12.6 us
    unnamed x3, matrix products  11.6 us
    squeeze x1, local copies, waits for them, and re-layouts, local(): w_keyval[0]  7.62 us
    all_gather x1, waiting for transfers between devices, local(): lax.all_gather(own_half, ('ctx', 'tp'), axis=0, tiled=False)  6.88 us
  transfers between devices with their start and end apart: 4, of which 4 were waited for; matrix products, arithmetic and copies ran while one was open for 20% of the time, Pallas kernels for 0%

profile of v1, /device:TPU:0, one launch (start us, length us, event | category | flops | bytes accessed | tf_op | source)
XLA Modules:
  0.0 229.3 jit_solution(13577743396579141682)
XLA Ops:
  6.6 1.2 convert_reduce_fusion
  7.8 1.2 fusion.28
  9.1 1.9 fusion.32
  11.0 0.1 broadcast_compare_fusion
  11.1 0.3 fusion.96
  11.5 2.5 %convolution_bitcast_fusion = f32[128,1280]{1,0:T(8,128)} fusion(bf16[4,80,1280]{2,1,0:T(8,128)(2,1)} %param.21, f32[4,128,128]{1,2,0:T(8,128)S(1)} %get-tuple-element.22, f32[4,128]{1,0:T(4,128)S(1)} %get-tuple-element.21, bf16[128,3,4,80]{0,3,2,1:T(8,128)(2,1)S(1)} %convert_element_type.68, f32[128,4]{0,1:T(4,128)S(1)} %bitcast.113), kind=kOutput, calls=%fused_computation.10 | convolution fusion | flops 115556352 | bytes 1822720 | tf_op jit(solution)/shard_map/phd,hdf->pf/dot_general | solution.py:109
  14.3 0.7 fusion.50
  15.0 0.7 fusion.94
  15.7 0.1 select_reduce_fusion.2
  15.8 26.6 %all-gather.8.cloned.1.call-done = f32[512,1280]{1,0:T(8,128)} async-done(((f32[128,1280]{1,0:T(8,128)}), f32[512,1280]{1,0:T(8,128)}) %all-gather.8.cloned.1.call-update) | async-done | bytes 2621456 | tf_op jit(solution)/shard_map/all_gather | solution.py:110
  42.4 2.0 reduce_sum.161
  44.4 0.1 fusion.47
  44.6 0.2 multiply_reduce_fusion
  44.8 0.9 add_convert_fusion
  45.7 1.2 reshape.665
  46.9 0.2 convolution_convert_fusion
  47.2 16.6 %all_to_all.5 = bf16[8,32,640]{2,1,0:T(8,128)(2,1)S(1)} all-to-all(bf16[8,32,640]{2,1,0:T(8,128)(2,1)S(1)} %bitcast.104), channel_id=1, replica_groups=mesh['vis'=2,'ctx'=8,'tp'=2] {'ctx'}, dimensions={0} | all-to-all | bytes 655360 | tf_op jit(solution)/shard_map/all_to_all | solution.py:129
  63.8 0.1 copy.88
  63.9 0.1 copy.89
  64.2 2.9 %fusion.97 = f32[256,1024]{1,0:T(8,128)} fusion(bf16[256,640]{1,0:T(8,128)(2,1)S(1)} %reshape.668, bf16[640,1024]{1,0:T(8,128)(2,1)} %param.24), kind=kOutput, calls=%fused_computation.190 | convolution fusion | flops 335544320 | bytes 2686976 | tf_op jit(solution)/shard_map/dot_general | solution.py:133
  67.4 0.1 and.279
  67.7 0.3 fusion.95
  67.9 61.3 %reduce-scatter.2.cloned.1.call-done = f32[32,1024]{1,0:T(8,128)} async-done(((f32[256,1024]{1,0:T(8,128)}), f32[32,1024]{1,0:T(8,128)}) %reduce-scatter.2.cloned.1.call-update) | async-done | bytes 131088 | tf_op jit(solution)/shard_map/reduce_scatter | solution.py:134
  129.3 1.9 fusion.16
  131.1 0.2 all-gather.10.cloned.1.call-start
  131.4 0.1 select_reduce_fusion.3
  131.5 1.0 gather_fusion.1
  132.5 0.5 and_select_fusion.8
  133.0 7.6 %copy.90 = bf16[4096,4,128]{0,2,1:T(8,128)(2,1)} copy(bf16[4096,4,128]{2,1,0:T(4,128)(2,1)} %bitcast.98) | data formatting | bytes 8388608 | tf_op jit(solution)/shard_map/squeeze | solution.py:164
  140.7 0.2 multiply_cosine_fusion
  140.9 6.1 %all-gather.6.cloned.1.call-done = bf16[128,4096]{1,0:T(8,128)(2,1)} async-done(((bf16[128,1024]{1,0:T(8,128)(2,1)}), bf16[128,4096]{1,0:T(8,128)(2,1)}) %all-gather.6.cloned.1.call-update) | async-done | bytes 1048592 | tf_op jit(solution)/shard_map/all_gather | solution.py:148
  147.0 1.5 fusion.3
  148.5 3.8 %fusion.40 = f32[128,512]{0,1:S(1)} fusion(bf16[4096,512]{0,1:T(8,128)(2,1)} %bitcast.99, bf16[128,4096]{1,0:T(8,128)(2,1)} %all-gather.6.cloned.1.call-done, f32[4096]{0:T(1024)S(1)} %copy-done.8, f32[128]{0:T(128)S(1)} %add_rsqrt_fusion), kind=kOutput, calls=%fused_computation.50 | convolution fusion | flops 538968064 | bytes 5521920
  152.4 0.7 fusion.42
  153.1 21.3 %copy.92 = bf16[4096,4,2,128]{0,3,2,1:T(8,128)(2,1)} copy(bf16[4096,4,2,128]{3,2,1,0:T(2,128)(2,1)} %param.32) | data formatting | bytes 16777216 | tf_op args[15]
  174.6 4.5 %gather_fusion = s32[1024]{0:T(1024)S(1)} fusion(s32[1024]{0:T(1024)S(1)} %copy-done.1, s32[1024]{0:T(1024)S(1)} %broadcast_clamp_fusion), kind=kCustom, calls=%fused_computation | custom fusion | bytes 12288 | tf_op jit(solution)/shard_map/jit(_take)/gather | solution.py:176
  179.2 1.7 compare_and_fusion
  180.8 5.8 %fusion.38 = f32[128,1024]{0,1:S(1)} fusion(bf16[4096,1024]{0,1:T(8,128)(2,1)} %bitcast.97, bf16[128,4096]{1,0:T(8,128)(2,1)S(1)} %copy-done.3, f32[4096]{0:T(1024)} %param.31, f32[128]{0:T(128)} %copy-done.13), kind=kOutput, calls=%fused_computation.49 | convolution fusion | flops 1075838976 | bytes 9978368
  186.7 0.8 subtract_convert_fusion
  187.5 6.9 %all-gather.10.cloned.1.call-done = bf16[2048,4,128]{0,2,1:T(8,128)(2,1)} async-done(((bf16[128,4,128]{0,2,1:T(8,128)(2,1)}), bf16[2048,4,128]{0,2,1:T(8,128)(2,1)}) %all-gather.10.cloned.1.call-update) | async-done | bytes 2097168 | tf_op jit(solution)/shard_map/all_gather | solution.py:169
  194.3 4.4 %reshape.669 = bf16[8,2,128,4,128]{2,1,0,4,3:T(2,128)(2,1)} reshape(bf16[2048,4,128]{0,2,1:T(8,128)(2,1)} %all-gather.10.cloned.1.call-done) | data formatting | bytes 4194304 | tf_op jit(solution)/shard_map/reshape | solution.py:169
  198.8 6.8 %fusion.93 = (bf16[8,1,128,4,128]{2,1,0,4,3:T(2,128)(2,1)}, bf16[8,1,128,4,128]{2,1,0,4,3:T(2,128)(2,1)}) fusion(bf16[8,2,128,4,128]{2,1,0,4,3:T(2,128)(2,1)} %reshape.669), kind=kLoop, calls=%fused_computation.186 | loop fusion | bytes 4194304 | tf_op jit(solution)/shard_map/slice | solution.py:173
  205.6 5.8 %copy.91 = bf16[8,1,128,4,128]{4,2,0,3,1:T(8,128)(2,1)} copy(bf16[8,1,128,4,128]{2,1,0,4,3:T(2,128)(2,1)} %get-tuple-element.11) | data formatting | bytes 2097152 | tf_op jit(solution)/shard_map/slice | solution.py:173
  211.4 4.7 %copy.105 = bf16[8,1,128,4,128]{4,2,0,3,1:T(8,128)(2,1)S(1)} copy(bf16[8,1,128,4,128]{2,1,0,4,3:T(2,128)(2,1)} %get-tuple-element.12) | data formatting | bytes 2097152
  216.1 2.1 fusion.2
  218.2 0.9 fusion
  219.1 1.9 fusion.23
  221.0 1.8 copy.97
  (76 shorter events, 1.3 us)
Async XLA Ops:
  6.5 2.5 %copy-start = (bf16[1280,3,4,80]{0,3,2,1:T(8,128)(2,1)S(1)}, bf16[1280,3,4,80]{0,3,2,1:T(8,128)(2,1)}, u32[]{:S(2)}) copy-start(bf16[1280,3,4,80]{0,3,2,1:T(8,128)(2,1)} %param.20) | copy-start | bytes 7372804
  6.5 4.5 %copy-start.15 = (s32[128]{0:T(128)S(1)}, s32[128]{0:T(128)}, u32[]{:S(2)}) copy-start(s32[128]{0:T(128)} %param.26) | copy-start | bytes 1540
  6.5 7.5 %copy-start.12 = (s32[256]{0:T(256)S(1)}, s32[256]{0:T(256)}, u32[]{:S(2)}) copy-start(s32[256]{0:T(256)} %param.27) | copy-start | bytes 3076
  6.5 7.7 %copy-start.11 = (s32[8]{0:T(128)S(1)}, s32[8]{0:T(128)}, u32[]{:S(2)}) copy-start(s32[8]{0:T(128)} %param.28) | copy-start | bytes 100
  6.5 35.9 %all-gather.8.cloned.1.call-start = ((), (), s32[]{:S(2)}) async-start(), calls=%async_computation.4 | async-start | bytes 3276800 | tf_op jit(solution)/shard_map/all_gather | solution.py:110
  11.0 33.4 %copy-start.2 = (bf16[128,1280]{1,0:T(8,128)(2,1)S(1)}, bf16[128,1280]{1,0:T(8,128)(2,1)}, u32[]{:S(2)}) copy-start(bf16[128,1280]{1,0:T(8,128)(2,1)} %param.17) | copy-start | bytes 983044
  11.4 33.4 %copy-start.9 = (f32[1280]{0:T(1024)S(1)}, f32[1280]{0:T(1024)}, u32[]{:S(2)}) copy-start(f32[1280]{0:T(1024)} %param.23) | copy-start | bytes 15364
  11.4 33.4 %copy-start.10 = (f32[1280]{0:T(1024)S(1)}, f32[1280]{0:T(1024)}, u32[]{:S(2)}) copy-start(f32[1280]{0:T(1024)} %param.22) | copy-start | bytes 15364
  14.0 115.2 %reduce-scatter.2.cloned.1.call-start = ((), (), s32[]{:S(2)}) async-start(), calls=%async_computation.2 | async-start | bytes 1179648 | tf_op jit(solution)/shard_map/reduce_scatter | solution.py:134
  45.7 21.6 %copy-start.16 = (s32[8,2]{0,1:T(2,128)S(1)}, s32[8,2]{0,1:T(2,128)}, u32[]{:S(2)}) copy-start(s32[8,2]{0,1:T(2,128)} %param.25) | copy-start | bytes 196
  45.7 83.5 %copy-start.7 = (bf16[128,1024]{1,0:T(8,128)(2,1)S(1)}, bf16[128,1024]{1,0:T(8,128)(2,1)}, u32[]{:S(2)}) copy-start(bf16[128,1024]{1,0:T(8,128)(2,1)} %param.30) | copy-start | bytes 786436
  47.2 84.3 %copy-start.1 = (s32[1024]{0:T(1024)S(1)}, s32[1024]{0:T(1024)}, u32[]{:S(2)}) copy-start(s32[1024]{0:T(1024)} %param.29) | copy-start | bytes 12292
  67.1 79.9 %all-gather.6.cloned.1.call-start = ((), (), s32[]{:S(2)}) async-start(), calls=%async_computation.3 | async-start | bytes 1310720 | tf_op jit(solution)/shard_map/all_gather | solution.py:148
  131.1 63.2 %all-gather.10.cloned.1.call-start = ((), (), s32[]{:S(2)}) async-start(), calls=%async_computation.5 | async-start | bytes 2228224 | tf_op jit(solution)/shard_map/all_gather | solution.py:169
  133.0 7.6 %copy-start.14 = (s32[128]{0:T(128)}, s32[128]{0:T(128)S(1)}, u32[]{:S(2)}) copy-start(s32[128]{0:T(128)S(1)} %get-tuple-element.10) | copy-start | bytes 1540
  133.0 15.5 %copy-start.8 = (f32[4096]{0:T(1024)S(1)}, f32[4096]{0:T(1024)}, u32[]{:S(2)}) copy-start(f32[4096]{0:T(1024)} %param.31) | copy-start | bytes 49156
  140.9 12.3 %copy-start.5 = (f32[128,64]{0,1:T(8,128)}, f32[128,64]{0,1:T(8,128)S(1)}, u32[]{:S(2)}) copy-start(f32[128,64]{0,1:T(8,128)S(1)} %get-tuple-element.18) | copy-start | bytes 98308
  148.5 26.0 %copy-start.13 = (f32[128]{0:T(128)}, f32[128]{0:T(128)S(1)}, u32[]{:S(2)}) copy-start(f32[128]{0:T(128)S(1)} %add_rsqrt_fusion) | copy-start | bytes 1540
  174.5 6.3 %copy-start.3 = (bf16[128,4096]{1,0:T(8,128)(2,1)S(1)}, bf16[128,4096]{1,0:T(8,128)(2,1)}, u32[]{:S(2)}) copy-start(bf16[128,4096]{1,0:T(8,128)(2,1)} %all-gather.6.cloned.1.call-done) | copy-start | bytes 3145732
  180.8 5.8 %copy-start.6 = (f32[128,64]{0,1:T(8,128)S(1)}, f32[128,64]{0,1:T(8,128)}, u32[]{:S(2)}) copy-start(f32[128,64]{0,1:T(8,128)} %copy-done.5) | copy-start | bytes 98308
  216.1 2.1 copy-start.4
Sparse Core Ops, SparseCore 0:
  14.1 28.2 all-gather.7
  67.2 61.9 reduce-scatter.1
  131.3 15.6 all-gather.5
  153.3 41.0 all-gather.9
